TPU v7x, 32 devices: a whole 2x2x4 slice. The times are simulated.
32 devices in a mesh: space: 8 (over z, x), fsdp: 4 (over y, core).
Axes of the slice: x: 2, y: 2, z: 4, core: 2. Of those that a mesh axis runs over, the one named last changes fastest.
Arguments:
- features: bfloat16 [4, 128, 8, 8, 512], P('fsdp', 'space'), may hold values from -6 to 6
- cotangent: bfloat16 [4, 128, 8, 8, 512], P('fsdp', 'space'), may hold values from -6 to 6
- tissue: int32 [4, 128], P('fsdp', 'space'), may hold values 0 or 1
- weight: bfloat16 [27, 64, 64], P(None, 'fsdp'), may hold values from -0.15625 to 0.15625
Outputs:
- activations: bfloat16 [4, 128, 8, 8, 512], P('fsdp', 'space')
- input_grad: bfloat16 [4, 128, 8, 8, 512], P('fsdp', 'space')
- weight_grad: float32 [27, 64, 64], P(None, 'fsdp')
All inputs are finite; a program needn't handle non-finite values. No bound on the sum of `tissue` on one device may be relied on, other than what follows from the above.
Results may differ from a plain program's by a relative error of at most 0.0034.
Values may be sent and summed in bfloat16 or wider, within the bound.
No kernel may reach another device: no remote copies, remote signals or barrier semaphores. Data moves between devices by JAX's collectives and lax.ppermute only.
A program may use at most 192 MiB of HBM per device.

v0:
```python
import math
import jax
import jax.numpy as jnp
from jax import lax
from jax.sharding import PartitionSpec as P

BRICK_X = 2
BRICK_Y = 2
BRICK_Z = 4
PAIR = 2
DEPTH = 2
CONV_DIMS = ("NDHWC", "DHWIO", "NDHWC")


def from_behind(shard, axis, by):
    peers = lax.axis_size(axis)
    pairs = [(i, i + by) for i in range(peers) if 0 <= i + by < peers]
    return lax.ppermute(shard, axis, pairs)


def grid_shape(number):
    factors = [1, 1, 1]
    places = 0
    while number % 2 == 0:
        factors[places % 3] = factors[places % 3] * 2
        number = number // 2
        places = places + 1
    factors[0] = factors[0] * number
    return factors


def to_volume(bricks, edge_cells, lanes):
    per_brick = edge_cells // PAIR
    blocks = bricks.reshape(BRICK_X, BRICK_Y, BRICK_Z, edge_cells, edge_cells, per_brick, lanes)
    blocks = blocks.transpose(0, 3, 1, 4, 2, 5, 6)
    return blocks.reshape(BRICK_X * edge_cells, BRICK_Y * edge_cells, BRICK_Z * per_brick, lanes)


def to_bricks(volume, edge_cells, lanes):
    per_brick = edge_cells // PAIR
    blocks = volume.reshape(BRICK_X, edge_cells, BRICK_Y, edge_cells, BRICK_Z, per_brick, lanes)
    blocks = blocks.transpose(0, 2, 4, 1, 3, 5, 6)
    return blocks.reshape(BRICK_X * BRICK_Y * BRICK_Z, edge_cells, edge_cells, per_brick * lanes)


def neighbour_plane(portion, offset, present):
    arrived = from_behind(portion, "space", offset)
    return jnp.where(present, arrived, jnp.zeros_like(arrived))


def extend(volume, grid_dims, places, widths):
    strides = (grid_dims[1] * grid_dims[2], grid_dims[2], 1)
    for axis_pos in range(3):
        axis = axis_pos + 1
        extent = volume.shape[axis]
        width = widths[axis_pos]
        last_layer = lax.slice_in_dim(volume, extent - width, extent, axis=axis)
        first_layer = lax.slice_in_dim(volume, 0, width, axis=axis)
        from_below = neighbour_plane(last_layer, strides[axis_pos], places[axis_pos] > 0)
        from_above = neighbour_plane(
            first_layer, -strides[axis_pos], places[axis_pos] < grid_dims[axis_pos] - 1
        )
        volume = jnp.concatenate([from_below, volume, from_above], axis=axis)
    return volume


def super_kernel(weight_full, channels):
    taps = weight_full.reshape(3, 3, 3, channels, channels)
    zero = jnp.zeros((3, 3, channels, channels), weight_full.dtype)
    rows = []
    for dz in range(3):
        row = []
        for hi in range(PAIR):
            col = []
            for ho in range(PAIR):
                c = 2 * dz - 1 + hi - ho
                col.append(taps[:, :, c] if 0 <= c < 3 else zero)
            row.append(jnp.concatenate(col, axis=-1))
        rows.append(jnp.concatenate(row, axis=-2))
    return jnp.stack(rows, axis=2)


def fold_kernel_grad(grad_sup, channels):
    taps = [None, None, None]
    for dz in range(3):
        for hi in range(PAIR):
            for ho in range(PAIR):
                c = 2 * dz - 1 + hi - ho
                if 0 <= c < 3:
                    block = grad_sup[
                        :,
                        :,
                        dz,
                        hi * channels : (hi + 1) * channels,
                        ho * channels : (ho + 1) * channels,
                    ]
                    taps[c] = block if taps[c] is None else taps[c] + block
    return jnp.stack(taps, axis=2).reshape(27, channels, channels)


def conv(volume, kernel):
    return lax.conv_general_dilated(
        volume[None],
        kernel,
        (1, 1, 1),
        "VALID",
        dimension_numbers=CONV_DIMS,
        preferred_element_type=jnp.float32,
    )[0]


def kernel_grad(inputs, grads):
    out = lax.conv_general_dilated(
        inputs[None],
        grads[None],
        (1, 1, 1),
        "VALID",
        dimension_numbers=("CDHWN", "IDHWO", "NDHWC"),
        preferred_element_type=jnp.float32,
    )
    return out.transpose(1, 2, 3, 0, 4)


def local(features, cotangent, tissue, weight):
    edge_cells = features.shape[2]
    channels = weight.shape[2]
    lanes = PAIR * channels
    grid_dims = grid_shape(lax.axis_size("space"))
    index_now = lax.axis_index("space")
    places = (
        index_now // (grid_dims[1] * grid_dims[2]),
        index_now // grid_dims[2] % grid_dims[1],
        index_now % grid_dims[2],
    )
    weight_full = lax.all_gather(weight, "fsdp", axis=1, tiled=True)
    k_fwd = super_kernel(weight_full, channels)
    k_back = jnp.flip(k_fwd, (0, 1, 2)).transpose(0, 1, 2, 4, 3)
    present = tissue[0][:, None, None, None] > 0
    inputs = features[0]
    incoming = cotangent[0]
    masked = jnp.where(present, inputs, jnp.zeros_like(inputs))
    masked_cot = jnp.where(present, incoming, jnp.zeros_like(incoming))
    both = jnp.stack(
        [to_volume(masked, edge_cells, lanes), to_volume(masked_cot, edge_cells, lanes)]
    )
    grown = extend(both, grid_dims, places, (DEPTH, DEPTH, 1))
    grown = jnp.pad(grown, ((0, 0), (0, 0), (0, 0), (1, 1), (0, 0)))
    padded_in = grown[0]
    cot_ext = grown[1, 1:-1, 1:-1, 1:-1]
    pre_ext = conv(padded_in, k_fwd)
    gate_ext = jax.nn.sigmoid(pre_ext)
    slope_ext = gate_ext * (1.0 + pre_ext * (1.0 - gate_ext))
    grad_ext = (cot_ext.astype(jnp.float32) * slope_ext).astype(jnp.bfloat16)
    tissue_mask = tissue[0].astype(jnp.float32)[:, None, None, None]
    pre = to_bricks(pre_ext[1:-1, 1:-1, 1:-1], edge_cells, lanes)
    gate_val = to_bricks(gate_ext[1:-1, 1:-1, 1:-1], edge_cells, lanes)
    activations = (tissue_mask * (inputs.astype(jnp.float32) + pre * gate_val)).astype(jnp.bfloat16)
    back = to_bricks(conv(grad_ext, k_back), edge_cells, lanes)
    input_grad = (tissue_mask * (incoming.astype(jnp.float32) + back)).astype(jnp.bfloat16)
    total_cells = (
        lax.axis_size("space") * lax.axis_size("fsdp") * BRICK_X * BRICK_Y * BRICK_Z * edge_cells**3
    )
    grad_sup = kernel_grad(padded_in[1:-1, 1:-1, 1:-1], grad_ext[1:-1, 1:-1, 1:-1])
    grad_term = fold_kernel_grad(grad_sup, channels) / math.sqrt(total_cells)
    grad_part = lax.psum_scatter(grad_term, "fsdp", scatter_dimension=1, tiled=True)
    grad_part = lax.psum(grad_part, "space")
    return (activations[None], input_grad[None], grad_part)


def solution(mesh):
    return jax.shard_map(
        local,
        mesh=mesh,
        in_specs=(
            P("fsdp", "space", None, None, None),
            P("fsdp", "space", None, None, None),
            P("fsdp", "space"),
            P(None, "fsdp", None),
        ),
        out_specs=(
            P("fsdp", "space", None, None, None),
            P("fsdp", "space", None, None, None),
            P(None, "fsdp", None),
        ),
        check_vma=False,
    )
```

profile of v0, /device:TPU:0, one launch (start us, length us, event | category | flops | bytes accessed | tf_op | source)
XLA Modules:
  0.0 291.2 jit_solution(907447351510930595)
XLA Ops:
  8.0 2.7 copy_select_fusion.1
  12.0 6.7 %collective-permute-start = (bf16[2,2,16,16,128]{4,3,2,1,0:T(8,128)(2,1)S(1)}, bf16[2,2,16,16,128]{4,3,2,1,0:T(8,128)(2,1)S(1)}, u32[]{:S(2)}, u32[]{:S(2)}) collective-permute-start(bf16[2,2,16,16,128]{4,3,2,1,0:T(8,128)(2,1)S(1)} %get-tuple-element.11), channel_id=1, source_target_pairs={{0,16},{4,20},{8,24},{12,28},{1,17},{5,21},{9,25},{13,29},{2,18},{... | collective-permute-start | bytes 786440 | tf_op jit(solution)/shard_map/ppermute | solution.py:18
  18.7 7.7 %all_gather.3 = bf16[27,64,64]{2,1,0:T(8,128)(2,1)S(1)} all-gather(bf16[27,16,64]{2,1,0:T(8,128)(2,1)S(1)} %copy-done.14), channel_id=1, replica_groups=mesh['space'=8,'fsdp'=4] {'fsdp'}, dimensions={1}, use_global_device_ids=true | all-gather | bytes 276480 | tf_op jit(solution)/shard_map/all_gather | solution.py:135
  26.4 1.7 collective-permute-done.1
  30.6 4.8 %collective-permute-start.2 = (bf16[2,20,2,16,128]{4,3,2,1,0:T(8,128)(2,1)S(1)}, bf16[2,20,2,16,128]{4,3,2,1,0:T(8,128)(2,1)S(1)}, u32[]{:S(2)}, u32[]{:S(2)}) collective-permute-start(bf16[2,20,2,16,128]{4,3,2,1,0:T(8,128)(2,1)S(1)} %get-tuple-element.9), channel_id=1, source_target_pairs={{0,8},{4,12},{8,16},{12,20},{16,24},{20,28},{1,9},{5,13},{9,17},{1... | collective-permute-start | bytes 983048 | tf_op jit(solution)/shard_map/ppermute | solution.py:18
  35.7 5.6 %collective-permute-done.3 = bf16[2,20,2,16,128]{4,3,2,1,0:T(8,128)(2,1)S(1)} collective-permute-done((bf16[2,20,2,16,128]{4,3,2,1,0:T(8,128)(2,1)S(1)}, bf16[2,20,2,16,128]{4,3,2,1,0:T(8,128)(2,1)S(1)}, u32[]{:S(2)}, u32[]{:S(2)}) %collective-permute-start.3) | collective-permute-done | bytes 327712 | tf_op jit(solution)/shard_map/ppermute | solution.py:18
  42.5 1.9 pad_maximum_fusion.7
  46.2 4.7 %collective-permute-start.4 = (bf16[2,20,20,1,128]{4,3,2,1,0:T(2,128)(2,1)S(1)}, bf16[2,20,20,1,128]{4,3,2,1,0:T(2,128)(2,1)S(1)}, u32[]{:S(2)}, u32[]{:S(2)}) collective-permute-start(bf16[2,20,20,1,128]{4,3,2,1,0:T(2,128)(2,1)S(1)} %get-tuple-element.7), channel_id=1, source_target_pairs={{0,4},{4,8},{8,12},{12,16},{16,20},{20,24},{24,28},{1,5},{5,9},{9,... | collective-permute-start | bytes 614408 | tf_op jit(solution)/shard_map/ppermute | solution.py:18
  50.9 6.3 %collective-permute-done.5 = bf16[2,20,20,1,128]{4,3,2,1,0:T(2,128)(2,1)S(1)} collective-permute-done((bf16[2,20,20,1,128]{4,3,2,1,0:T(2,128)(2,1)S(1)}, bf16[2,20,20,1,128]{4,3,2,1,0:T(2,128)(2,1)S(1)}, u32[]{:S(2)}, u32[]{:S(2)}) %collective-permute-start.5) | collective-permute-done | bytes 204832 | tf_op jit(solution)/shard_map/ppermute | solution.py:18
  57.7 8.5 %collective-permute-done.4 = bf16[2,20,20,1,128]{4,3,2,1,0:T(2,128)(2,1)S(1)} collective-permute-done((bf16[2,20,20,1,128]{4,3,2,1,0:T(2,128)(2,1)S(1)}, bf16[2,20,20,1,128]{4,3,2,1,0:T(2,128)(2,1)S(1)}, u32[]{:S(2)}, u32[]{:S(2)}) %collective-permute-start.4) | collective-permute-done | bytes 204832 | tf_op jit(solution)/shard_map/ppermute | solution.py:18
  66.6 5.9 %pad_maximum_fusion = bf16[2,20,20,18,128]{4,3,2,1,0:T(8,128)(2,1)S(1)} fusion(bf16[2,20,20,1,128]{4,3,2,1,0:T(2,128)(2,1)S(1)} %broadcast_select_fusion.1, bf16[2,20,2,16,128]{4,3,2,1,0:T(8,128)(2,1)S(1)} %broadcast_select_fusion.3, bf16[2,2,16,16,128]{4,3,2,1,0:T(8,128)(2,1)S(1)} %broadcast_select_fusion.5, bf16[1,16,16,16,128]{4,3,2,1,0:T(8,128)(2,1)S(1)} %bitcast.89, ...), kind=kLoop, calls=%fused_computation.6 | loop fusion | flops 29491200 | bytes 7372800 | tf_op jit(solution)/shard_map/concatenate | solution.py:63
  72.5 3.0 %fusion.29 = (bf16[20,20,20,128]{3,2,1,0:T(8,128)(2,1)}, bf16[20,20,1,20,128]{4,3,1,0,2:T(8,128)(2,1)S(1)}) fusion(bf16[2,20,20,18,128]{4,3,2,1,0:T(8,128)(2,1)S(1)} %pad_maximum_fusion), kind=kLoop, calls=%fused_computation.39 | loop fusion | bytes 7782400 | tf_op jit(solution)/shard_map/squeeze | solution.py:148
  77.5 17.0 %add_multiply_fusion = (f32[18,18,8,3,128]{4,2,3,1,0:T(8,128)}, f32[18,18,8,3,128]{4,2,3,1,0:T(8,128)S(1)}) fusion(bf16[3,3,1,128,128]{4,3,2,1,0:T(8,128)(2,1)S(1)} %get-tuple-element.21, bf16[3,3,1,128,128]{4,3,2,1,0:T(8,128)(2,1)S(1)} %get-tuple-element.20, bf16[3,3,1,128,128]{4,3,2,1,0:T(8,128)(2,1)S(1)} %get-tuple-element.19, ...), kind=kOutput, calls=%fused_computation.17 | convolution fusion | flops 6900842496 | bytes 12738584 | tf_op jit(solution)/shard_map/conv_general_dilated | solution.py:102
  94.4 4.0 %copy.40 = f32[18,18,8,3,128]{4,3,2,1,0:T(4,128)} copy(f32[18,18,8,3,128]{4,2,3,1,0:T(8,128)S(1)} %get-tuple-element.27) | data formatting | bytes 7962624 | tf_op jit(solution)/shard_map/conv_general_dilated | solution.py:102
  98.4 7.3 %reshape.72 = f32[18,18,1,24,128]{4,3,1,0,2:T(8,128)} reshape(f32[18,18,8,3,128]{4,3,2,1,0:T(4,128)} %copy.40) | data formatting | bytes 7962624 | tf_op jit(solution)/shard_map/conv_general_dilated | solution.py:102
  105.7 4.5 %slice_bitcast_fusion.1 = f32[18,18,18,128]{3,2,1,0:T(8,128)} fusion(f32[18,18,1,24,128]{4,3,1,0,2:T(8,128)} %reshape.72), kind=kLoop, calls=%fused_computation.16 | loop fusion | bytes 5971968 | tf_op jit(solution)/shard_map/squeeze | solution.py:102
  110.2 3.0 %add_divide_fusion = f32[18,18,18,128]{3,2,1,0:T(8,128)} fusion(f32[18,18,1,24,128]{4,3,1,0,2:T(8,128)S(1)} %copy-done.1), kind=kLoop, calls=%fused_computation.18 | loop fusion | flops 2239488 | bytes 5971968 | tf_op jit(solution)/shard_map/div | solution.py:151
  113.2 3.9 %convert_bitcast_fusion = f32[18,18,18,128]{3,2,1,0:T(8,128)} fusion(bf16[2,20,20,18,128]{4,3,2,1,0:T(8,128)(2,1)} %copy-done), kind=kLoop, calls=%fused_computation.4 | loop fusion | flops 746496 | bytes 4478976 | tf_op jit(solution)/shard_map/convert_element_type | solution.py:153
  117.1 4.0 %copy.42 = f32[18,18,8,3,128]{4,3,2,1,0:T(4,128)} copy(f32[18,18,8,3,128]{4,2,3,1,0:T(8,128)S(1)} %copy-done.9) | data formatting | bytes 7962624 | tf_op jit(solution)/shard_map/mul | solution.py:152
  121.0 7.3 %reshape.81 = f32[18,18,1,24,128]{4,3,1,0,2:T(8,128)} reshape(f32[18,18,8,3,128]{4,3,2,1,0:T(4,128)} %copy.42) | data formatting | bytes 7962624 | tf_op jit(solution)/shard_map/mul | solution.py:152
  128.3 3.2 %fusion.22 = bf16[18,18,1,18,128]{4,3,1,0,2:T(8,128)(2,1)S(1)} fusion(f32[18,18,1,24,128]{4,3,1,0,2:T(8,128)} %reshape.81, bf16[2,20,20,18,128]{4,3,2,1,0:T(8,128)(2,1)} %copy-done), kind=kLoop, calls=%fused_computation.33 | loop fusion | flops 2239488 | bytes 5971968 | tf_op jit(solution)/shard_map/convert_element_type | solution.py:153
  131.5 1.6 pad.11
  133.1 5.5 %reshape.75 = bf16[18,18,1,8,3,128]{5,4,3,1,0,2:T(4,128)(2,1)S(1)} reshape(bf16[18,18,1,24,128]{4,3,1,0,2:T(8,128)(2,1)} %pad.11) | data formatting | bytes 3981312 | tf_op jit(solution)/shard_map/conv_general_dilated | solution.py:102
  140.3 1.5 slice.102
  144.1 4.3 %fusion.31 = (bf16[1,16,16,16,128]{4,3,2,1,0:T(8,128)(2,1)S(1)}, f32[16,16,16,128]{3,2,1,0:T(8,128)}) fusion(f32[18,18,18,128]{3,2,1,0:T(8,128)S(1)} %copy-done.2, f32[18,18,18,128]{3,2,1,0:T(8,128)S(1)} %copy-done.3, f32[18,18,18,128]{3,2,1,0:T(8,128)} %convert_bitcast_fusion), kind=kLoop, calls=%fused_computation.41 | loop fusion | flops 3670016 | bytes 9437184 | tf_op jit(solution)/shard_map/broadcast_in_dim | solution.py:115
  148.4 32.2 %fusion.17 = f32[3,3,3,128,128]{4,3,2,1,0:T(8,128)S(1)} fusion(bf16[1,18,18,18,128]{4,3,2,1,0:T(8,128)(2,1)S(1)} %slice_bitcast_fusion.2, bf16[1,16,16,16,128]{4,3,2,1,0:T(8,128)(2,1)S(1)} %get-tuple-element.3), kind=kOutput, calls=%fused_computation.25 | convolution fusion | flops 3623878656 | bytes 4311040 | tf_op jit(solution)/shard_map/transpose | solution.py:121
  182.9 13.3 %fusion.25 = f32[16,16,8,3,128]{4,2,3,1,0:T(8,128)S(1)} fusion(bf16[18,18,1,7,2,128]{5,3,4,1,0,2:T(8,128)(2,1)S(1)} %copy-done.10, bf16[18,18,1,8,3,128]{5,3,4,1,0,2:T(8,128)(2,1)S(1)} %copy-done.7, pred[8,3]{0,1:T(4,128)(4,1)S(1)} %copy-done.17, bf16[3,3,1,128,128]{4,3,2,1,0:T(8,128)(2,1)} %copy-done.13, bf16[3,3,1,128,128]{4,3,2,1,0:T(8,128)(2,1)} %copy-done.12, ...), kind=kOutput, calls=%fused_computation.37 | convolution fusion | flops 5447442432 | bytes 7182360 | tf_op jit(solution)/shard_map/conv_general_dilated | solution.py:102
  198.4 2.0 copy.41
  200.4 7.6 %reduce-scatter.2.cloned.1.call-done = f32[27,16,64]{2,1,0:T(8,128)} async-done(((f32[27,64,64]{2,1,0:T(8,128)}), f32[27,16,64]{2,1,0:T(8,128)}) %reduce-scatter.2.cloned.1.call-update) | async-done | bytes 110608 | tf_op jit(solution)/shard_map/reduce_scatter | solution.py:165
  208.1 4.2 %multiply_convert_fusion = (bf16[1,16,8,8,512]{4,3,2,1,0:T(8,128)(2,1)}, bf16[1,16,8,8,512]{4,3,2,1,0:T(8,128)(2,1)}) fusion(f32[1,16,8,8,512]{4,3,2,1,0:T(8,128)S(1)} %bitcast.94, bf16[1,16,8,8,512]{4,3,2,1,0:T(8,128)(2,1)} %param.5, f32[16]{0:T(128)S(1)} %copy-done.15, f32[1,16,8,8,512]{4,3,2,1,0:T(8,128)} %bitcast.95, ...), kind=kLoop, calls=%fused_computation.29 | loop fusion | flops 4194304 | bytes 8388672 | tf_op jit(solution)/shard_map/convert_element_type | solution.py:159
  212.3 70.0 %all-reduce.7.cloned.1.call-done = f32[27,16,64]{2,1,0:T(8,128)} async-done(((f32[27,16,64]{2,1,0:T(8,128)}), f32[27,16,64]{2,1,0:T(8,128)}) %all-reduce.7.cloned.1.call-update) | async-done | bytes 110608 | tf_op jit(solution)/shard_map/psum | solution.py:166
  282.2 1.6 copy.60
  (71 shorter events, 19.0 us)
Async XLA Ops:
  7.2 11.5 %copy-start.14 = (bf16[27,16,64]{2,1,0:T(8,128)(2,1)S(1)}, bf16[27,16,64]{2,1,0:T(8,128)(2,1)}, u32[]{:S(2)}) copy-start(bf16[27,16,64]{2,1,0:T(8,128)(2,1)} %param.7) | copy-start | bytes 165892
  7.2 200.8 %reduce-scatter.2.cloned.1.call-start = ((), (), s32[]{:S(2)}) async-start(), calls=%async_computation.1 | async-start | bytes 1105920 | tf_op jit(solution)/shard_map/reduce_scatter | solution.py:165
  10.7 17.4 %collective-permute-start.1 = (bf16[2,2,16,16,128]{4,3,2,1,0:T(8,128)(2,1)S(1)}, bf16[2,2,16,16,128]{4,3,2,1,0:T(8,128)(2,1)}, u32[]{:S(2)}, u32[]{:S(2)}) collective-permute-start(bf16[2,2,16,16,128]{4,3,2,1,0:T(8,128)(2,1)S(1)} %get-tuple-element.12), channel_id=1, source_target_pairs={{16,0},{20,4},{24,8},{28,12},{17,1},{21,5},{25,9},{29,13},{18,2},{... | collective-permute-start | bytes 786440 | tf_op jit(solution)/shard_map/ppermute | solution.py:18
  12.0 17.0 %collective-permute-start = (bf16[2,2,16,16,128]{4,3,2,1,0:T(8,128)(2,1)S(1)}, bf16[2,2,16,16,128]{4,3,2,1,0:T(8,128)(2,1)S(1)}, u32[]{:S(2)}, u32[]{:S(2)}) collective-permute-start(bf16[2,2,16,16,128]{4,3,2,1,0:T(8,128)(2,1)S(1)} %get-tuple-element.11), channel_id=1, source_target_pairs={{0,16},{4,20},{8,24},{12,28},{1,17},{5,21},{9,25},{13,29},{2,18},{... | collective-permute-start | bytes 786440 | tf_op jit(solution)/shard_map/ppermute | solution.py:18
  29.2 16.5 %copy-start.16 = (s32[1,16]{1,0:T(1,128)S(1)}, s32[1,16]{1,0:T(1,128)}, u32[]{:S(2)}) copy-start(s32[1,16]{1,0:T(1,128)} %param.6) | copy-start | bytes 196
  29.2 12.0 %collective-permute-start.3 = (bf16[2,20,2,16,128]{4,3,2,1,0:T(8,128)(2,1)S(1)}, bf16[2,20,2,16,128]{4,3,2,1,0:T(8,128)(2,1)S(1)}, u32[]{:S(2)}, u32[]{:S(2)}) collective-permute-start(bf16[2,20,2,16,128]{4,3,2,1,0:T(8,128)(2,1)S(1)} %get-tuple-element.10), channel_id=1, source_target_pairs={{8,0},{12,4},{16,8},{20,12},{24,16},{28,20},{9,1},{13,5},{17,9},{2... | collective-permute-start | bytes 983048 | tf_op jit(solution)/shard_map/ppermute | solution.py:18
  30.6 11.9 %collective-permute-start.2 = (bf16[2,20,2,16,128]{4,3,2,1,0:T(8,128)(2,1)S(1)}, bf16[2,20,2,16,128]{4,3,2,1,0:T(8,128)(2,1)S(1)}, u32[]{:S(2)}, u32[]{:S(2)}) collective-permute-start(bf16[2,20,2,16,128]{4,3,2,1,0:T(8,128)(2,1)S(1)} %get-tuple-element.9), channel_id=1, source_target_pairs={{0,8},{4,12},{8,16},{12,20},{16,24},{20,28},{1,9},{5,13},{9,17},{1... | collective-permute-start | bytes 983048 | tf_op jit(solution)/shard_map/ppermute | solution.py:18
  35.6 41.8 %copy-start.11 = (bf16[3,3,1,128,128]{4,3,2,1,0:T(8,128)(2,1)}, bf16[3,3,1,128,128]{4,3,2,1,0:T(8,128)(2,1)S(1)}, u32[]{:S(2)}) copy-start(bf16[3,3,1,128,128]{4,3,2,1,0:T(8,128)(2,1)S(1)} %get-tuple-element.19) | copy-start | bytes 884740
  35.6 41.8 %copy-start.12 = (bf16[3,3,1,128,128]{4,3,2,1,0:T(8,128)(2,1)}, bf16[3,3,1,128,128]{4,3,2,1,0:T(8,128)(2,1)S(1)}, u32[]{:S(2)}) copy-start(bf16[3,3,1,128,128]{4,3,2,1,0:T(8,128)(2,1)S(1)} %get-tuple-element.20) | copy-start | bytes 884740
  35.6 41.8 %copy-start.13 = (bf16[3,3,1,128,128]{4,3,2,1,0:T(8,128)(2,1)}, bf16[3,3,1,128,128]{4,3,2,1,0:T(8,128)(2,1)S(1)}, u32[]{:S(2)}) copy-start(bf16[3,3,1,128,128]{4,3,2,1,0:T(8,128)(2,1)S(1)} %get-tuple-element.21) | copy-start | bytes 884740
  44.4 12.9 %collective-permute-start.5 = (bf16[2,20,20,1,128]{4,3,2,1,0:T(2,128)(2,1)S(1)}, bf16[2,20,20,1,128]{4,3,2,1,0:T(2,128)(2,1)S(1)}, u32[]{:S(2)}, u32[]{:S(2)}) collective-permute-start(bf16[2,20,20,1,128]{4,3,2,1,0:T(2,128)(2,1)S(1)} %get-tuple-element.8), channel_id=1, source_target_pairs={{4,0},{8,4},{12,8},{16,12},{20,16},{24,20},{28,24},{5,1},{9,5},{13... | collective-permute-start | bytes 614408 | tf_op jit(solution)/shard_map/ppermute | solution.py:18
  46.2 20.0 %collective-permute-start.4 = (bf16[2,20,20,1,128]{4,3,2,1,0:T(2,128)(2,1)S(1)}, bf16[2,20,20,1,128]{4,3,2,1,0:T(2,128)(2,1)S(1)}, u32[]{:S(2)}, u32[]{:S(2)}) collective-permute-start(bf16[2,20,20,1,128]{4,3,2,1,0:T(2,128)(2,1)S(1)} %get-tuple-element.7), channel_id=1, source_target_pairs={{0,4},{4,8},{8,12},{12,16},{16,20},{20,24},{24,28},{1,5},{5,9},{9,... | collective-permute-start | bytes 614408 | tf_op jit(solution)/shard_map/ppermute | solution.py:18
  72.5 3.0 %copy-start = (bf16[2,20,20,18,128]{4,3,2,1,0:T(8,128)(2,1)}, bf16[2,20,20,18,128]{4,3,2,1,0:T(8,128)(2,1)S(1)}, u32[]{:S(2)}) copy-start(bf16[2,20,20,18,128]{4,3,2,1,0:T(8,128)(2,1)S(1)} %pad_maximum_fusion) | copy-start | bytes 11059204
  76.6 0.8 copy-start.18
  105.7 4.5 %copy-start.1 = (f32[18,18,1,24,128]{4,3,1,0,2:T(8,128)S(1)}, f32[18,18,1,24,128]{4,3,1,0,2:T(8,128)}, u32[]{:S(2)}) copy-start(f32[18,18,1,24,128]{4,3,1,0,2:T(8,128)} %reshape.72) | copy-start | bytes 11943940
  113.2 3.9 %copy-start.9 = (f32[18,18,8,3,128]{4,2,3,1,0:T(8,128)S(1)}, f32[18,18,8,3,128]{4,2,3,1,0:T(8,128)}, u32[]{:S(2)}) copy-start(f32[18,18,8,3,128]{4,2,3,1,0:T(8,128)} %get-tuple-element.26) | copy-start | bytes 11943940
  138.7 3.2 %copy-start.5 = (bf16[20,20,20,128]{3,2,1,0:T(8,128)(2,1)S(1)}, bf16[20,20,20,128]{3,2,1,0:T(8,128)(2,1)}, u32[]{:S(2)}) copy-start(bf16[20,20,20,128]{3,2,1,0:T(8,128)(2,1)} %get-tuple-element.5) | copy-start | bytes 6144004
  138.7 4.3 %copy-start.3 = (f32[18,18,18,128]{3,2,1,0:T(8,128)S(1)}, f32[18,18,18,128]{3,2,1,0:T(8,128)}, u32[]{:S(2)}) copy-start(f32[18,18,18,128]{3,2,1,0:T(8,128)} %add_divide_fusion) | copy-start | bytes 8957956
  139.1 1.3 copy-start.6
  140.3 3.8 %copy-start.2 = (f32[18,18,18,128]{3,2,1,0:T(8,128)S(1)}, f32[18,18,18,128]{3,2,1,0:T(8,128)}, u32[]{:S(2)}) copy-start(f32[18,18,18,128]{3,2,1,0:T(8,128)} %slice_bitcast_fusion.1) | copy-start | bytes 8957956
  180.7 1.9 copy-start.7
  180.7 2.2 copy-start.10
  180.7 2.2 copy-start.17
  182.0 100.2 %all-reduce.7.cloned.1.call-start = ((), (), s32[]{:S(2)}) async-start(), calls=%async_computation.2 | async-start | bytes 442368 | tf_op jit(solution)/shard_map/psum | solution.py:166
  196.8 1.6 copy-start.4
  197.0 11.1 %copy-start.8 = (bf16[1,16,8,8,512]{4,3,2,1,0:T(8,128)(2,1)S(1)}, bf16[1,16,8,8,512]{4,3,2,1,0:T(8,128)(2,1)}, u32[]{:S(2)}) copy-start(bf16[1,16,8,8,512]{4,3,2,1,0:T(8,128)(2,1)} %param.4) | copy-start | bytes 3145732
  197.0 11.1 %copy-start.15 = (f32[16]{0:T(128)S(1)}, f32[16]{0:T(128)}, u32[]{:S(2)}) copy-start(f32[16]{0:T(128)} %convert_bitcast_fusion.1) | copy-start | bytes 196
Sparse Core Ops, SparseCore 0:
  182.2 25.7 reduce-scatter.1
  211.4 70.8 all-reduce.6
where the time goes:
time: 296 us; the launch traced here: 291 us
  waiting for transfers between devices  101 us (34%)
  matrix products  62.5 us (21%)
  local copies, waits for them, and re-layouts  51 us (17%)
  other arithmetic  33.8 us (11%)
  starting transfers between devices  20.3 us (7%)
  between operations  14.9 us (5%)
  blocking collectives  7.7 us (3%)
    psum x1, waiting for transfers between devices, local(): grad_part = lax.psum(grad_part, 'space')  70 us
    transpose x1, matrix products, kernel_grad(): return out.transpose(1, 2, 3, 0, 4)  32.2 us
    conv_general_dilated x2, matrix products, conv(): lax.conv_general_dilated(volume[None], kernel, (1, 1, 1), 'VALID', dimens...  30.3 us
    ppermute x6, waiting for transfers between devices, from_behind(): return lax.ppermute(shard, axis, pairs)  23.2 us
    conv_general_dilated x9, local copies, waits for them, and re-layouts, conv(): lax.conv_general_dilated(volume[None], kernel, (1, 1, 1), 'VALID', dimens...  20.1 us
    ppermute x6, starting transfers between devices, from_behind(): return lax.ppermute(shard, axis, pairs)  20 us
    mul x2, local copies, waits for them, and re-layouts, local(): slope_ext = gate_ext * (1.0 + pre_ext * (1.0 - gate_ext))  11.3 us
    all_gather x1, blocking collectives, local(): weight_full = lax.all_gather(weight, 'fsdp', axis=1, tiled=True)  7.7 us
  transfers between devices with their start and end apart: 8, of which 7 were waited for; matrix products, arithmetic and copies ran while one was open for 8% of the time, Pallas kernels for 0%

commit v1 on v0

--- a/solution.py
+++ b/solution.py
@@ -10,6 +10,28 @@
 PAIR = 2
 DEPTH = 2
 CONV_DIMS = ("NDHWC", "DHWIO", "NDHWC")
+
+
+def joined_along(blocks, dim):
+    lengths = list(blocks.shape[1:])
+    lengths[dim] *= blocks.shape[0]
+    return jnp.moveaxis(blocks, 0, dim).reshape(lengths)
+
+
+def ring_gather(value, axis, dim):
+    size = lax.axis_size(axis)
+    pairs = [(i, (i + 1) % size) for i in range(size)]
+    back = [(b, a) for a, b in pairs]
+    lower, upper = ([], [])
+    for step in range(size - 1):
+        if step % 2 == 0:
+            lower.append(lax.ppermute(lower[-1] if lower else value, axis, pairs))
+        else:
+            upper.append(lax.ppermute(upper[-1] if upper else value, axis, back))
+    tiles = jnp.stack([*lower[::-1], value, *upper])
+    shift = lax.axis_index(axis) - len(lower)
+    tiles = tiles[(jnp.arange(size) - shift) % size]
+    return joined_along(tiles, dim)
 
 
 def from_behind(shard, axis, by):
@@ -132,7 +154,7 @@
         index_now // grid_dims[2] % grid_dims[1],
         index_now % grid_dims[2],
     )
-    weight_full = lax.all_gather(weight, "fsdp", axis=1, tiled=True)
+    weight_full = ring_gather(weight, "fsdp", 1)
     k_fwd = super_kernel(weight_full, channels)
     k_back = jnp.flip(k_fwd, (0, 1, 2)).transpose(0, 1, 2, 4, 3)
     present = tissue[0][:, None, None, None] > 0

time: 296 us -> 299 us (1.010)
  blocking collectives: 7.7 us -> 0 us
  starting transfers between devices: 20.3 us -> 25.3 us
  waiting for transfers between devices: 101 us -> 106 us
    all_gather x1 -> x0, blocking collectives: 7.7 us -> none  [local(): weight_full = lax.all_gather(weight, 'fsdp', axis=1, tiled=True)]
    ppermute x6, waiting for transfers between devices: 23.2 us -> 28 us  [from_behind(): return lax.ppermute(shard, axis, pairs)]
    unnamed x40 -> x44, local copies, waits for them, and re-layouts: 6.21 us -> 4.51 us
  transfers between devices with their start and end apart: 8 -> 11, of which waited for: 7 -> 7; matrix products, arithmetic and copies ran while one was open for 8% -> 9% of each run, Pallas kernels for 0% -> 0%
where the time goes in v1:
time: 299 us; the launch traced here: 294 us
  waiting for transfers between devices  106 us (35%)
  matrix products  62.7 us (21%)
  local copies, waits for them, and re-layouts  49.5 us (17%)
  other arithmetic  35.8 us (12%)
  starting transfers between devices  25.3 us (8%)
  between operations  15 us (5%)
    psum x1, waiting for transfers between devices, local(): grad_part = lax.psum(grad_part, 'space')  70 us
    transpose x1, matrix products, kernel_grad(): return out.transpose(1, 2, 3, 0, 4)  32.2 us
    conv_general_dilated x2, matrix products, conv(): lax.conv_general_dilated(volume[None], kernel, (1, 1, 1), 'VALID', dimens...  30.5 us
    ppermute x6, waiting for transfers between devices, from_behind(): return lax.ppermute(shard, axis, pairs)  28 us
    ppermute x6, starting transfers between devices, from_behind(): return lax.ppermute(shard, axis, pairs)  22.4 us
    conv_general_dilated x9, local copies, waits for them, and re-layouts, conv(): lax.conv_general_dilated(volume[None], kernel, (1, 1, 1), 'VALID', dimens...  19.5 us
    mul x2, local copies, waits for them, and re-layouts, local(): slope_ext = gate_ext * (1.0 + pre_ext * (1.0 - gate_ext))  11.3 us
    reduce_scatter x1, waiting for transfers between devices, local(): lax.psum_scatter(grad_term, 'fsdp', scatter_dimension=1, tiled=True)  7.81 us
  transfers between devices with their start and end apart: 11, of which 7 were waited for; matrix products, arithmetic and copies ran while one was open for 9% of the time, Pallas kernels for 0%

profile of v1, /device:TPU:0, one launch (start us, length us, event | category | flops | bytes accessed | tf_op | source)
XLA Modules:
  0.0 294.0 jit_solution(140283622218548682)
XLA Ops:
  8.0 2.7 copy_select_fusion.1
  12.1 2.5 collective-permute-start.8
  14.5 5.2 %collective-permute-start = (bf16[2,2,16,16,128]{4,3,2,1,0:T(8,128)(2,1)S(1)}, bf16[2,2,16,16,128]{4,3,2,1,0:T(8,128)(2,1)S(1)}, u32[]{:S(2)}, u32[]{:S(2)}) collective-permute-start(bf16[2,2,16,16,128]{4,3,2,1,0:T(8,128)(2,1)S(1)} %get-tuple-element.11), channel_id=1, source_target_pairs={{0,16},{4,20},{8,24},{12,28},{1,17},{5,21},{9,25},{13,29},{2,18},{... | collective-permute-start | bytes 786440 | tf_op jit(solution)/shard_map/ppermute | solution.py:40
  20.3 7.7 %collective-permute-done.1 = bf16[2,2,16,16,128]{4,3,2,1,0:T(8,128)(2,1)S(1)} collective-permute-done((bf16[2,2,16,16,128]{4,3,2,1,0:T(8,128)(2,1)S(1)}, bf16[2,2,16,16,128]{4,3,2,1,0:T(8,128)(2,1)S(1)}, u32[]{:S(2)}, u32[]{:S(2)}) %collective-permute-start.1) | collective-permute-done | bytes 262176 | tf_op jit(solution)/shard_map/ppermute | solution.py:40
  30.4 8.8 %collective-permute-start.2 = (bf16[2,20,2,16,128]{4,3,2,1,0:T(8,128)(2,1)}, bf16[2,20,2,16,128]{4,3,2,1,0:T(8,128)(2,1)}, u32[]{:S(2)}, u32[]{:S(2)}) collective-permute-start(bf16[2,20,2,16,128]{4,3,2,1,0:T(8,128)(2,1)} %get-tuple-element.9), channel_id=1, source_target_pairs={{0,8},{4,12},{8,16},{12,20},{16,24},{20,28},{1,9},{5,13},{9,17},{1... | collective-permute-start | bytes 983048 | tf_op jit(solution)/shard_map/ppermute | solution.py:40
  41.6 3.1 %collective-permute-done.3 = bf16[2,20,2,16,128]{4,3,2,1,0:T(8,128)(2,1)} collective-permute-done((bf16[2,20,2,16,128]{4,3,2,1,0:T(8,128)(2,1)}, bf16[2,20,2,16,128]{4,3,2,1,0:T(8,128)(2,1)}, u32[]{:S(2)}, u32[]{:S(2)}) %collective-permute-start.3) | collective-permute-done | bytes 327712 | tf_op jit(solution)/shard_map/ppermute | solution.py:40
  46.7 1.9 pad_maximum_fusion.8
  50.3 4.6 %collective-permute-start.4 = (bf16[2,20,20,1,128]{4,3,2,1,0:T(2,128)(2,1)S(1)}, bf16[2,20,20,1,128]{4,3,2,1,0:T(2,128)(2,1)S(1)}, u32[]{:S(2)}, u32[]{:S(2)}) collective-permute-start(bf16[2,20,20,1,128]{4,3,2,1,0:T(2,128)(2,1)S(1)} %get-tuple-element.7), channel_id=1, source_target_pairs={{0,4},{4,8},{8,12},{12,16},{16,20},{20,24},{24,28},{1,5},{5,9},{9,... | collective-permute-start | bytes 614408 | tf_op jit(solution)/shard_map/ppermute | solution.py:40
  54.8 7.3 %collective-permute-done.5 = bf16[2,20,20,1,128]{4,3,2,1,0:T(2,128)(2,1)S(1)} collective-permute-done((bf16[2,20,20,1,128]{4,3,2,1,0:T(2,128)(2,1)S(1)}, bf16[2,20,20,1,128]{4,3,2,1,0:T(2,128)(2,1)S(1)}, u32[]{:S(2)}, u32[]{:S(2)}) %collective-permute-start.5) | collective-permute-done | bytes 204832 | tf_op jit(solution)/shard_map/ppermute | solution.py:40
  62.6 8.8 %collective-permute-done.4 = bf16[2,20,20,1,128]{4,3,2,1,0:T(2,128)(2,1)S(1)} collective-permute-done((bf16[2,20,20,1,128]{4,3,2,1,0:T(2,128)(2,1)S(1)}, bf16[2,20,20,1,128]{4,3,2,1,0:T(2,128)(2,1)S(1)}, u32[]{:S(2)}, u32[]{:S(2)}) %collective-permute-start.4) | collective-permute-done | bytes 204832 | tf_op jit(solution)/shard_map/ppermute | solution.py:40
  71.9 5.9 %pad_maximum_fusion = bf16[2,20,20,18,128]{4,3,2,1,0:T(8,128)(2,1)S(1)} fusion(bf16[2,20,20,1,128]{4,3,2,1,0:T(2,128)(2,1)S(1)} %broadcast_select_fusion.1, bf16[2,20,2,16,128]{4,3,2,1,0:T(8,128)(2,1)S(1)} %broadcast_select_fusion.3, bf16[2,2,16,16,128]{4,3,2,1,0:T(8,128)(2,1)S(1)} %broadcast_select_fusion.5, bf16[1,16,16,16,128]{4,3,2,1,0:T(8,128)(2,1)S(1)} %bitcast.96, ...), kind=kLoop, calls=%fused_computation.7 | loop fusion | flops 29491200 | bytes 7372800 | tf_op jit(solution)/shard_map/concatenate | solution.py:85
  77.8 3.0 %fusion.29 = (bf16[20,20,20,128]{3,2,1,0:T(8,128)(2,1)}, bf16[20,20,1,20,128]{4,3,1,0,2:T(8,128)(2,1)S(1)}) fusion(bf16[2,20,20,18,128]{4,3,2,1,0:T(8,128)(2,1)S(1)} %pad_maximum_fusion), kind=kLoop, calls=%fused_computation.40 | loop fusion | bytes 7782400 | tf_op jit(solution)/shard_map/squeeze | solution.py:170
  82.8 17.2 %add_multiply_fusion = (f32[18,18,8,3,128]{4,2,3,1,0:T(8,128)}, f32[18,18,8,3,128]{4,2,3,1,0:T(8,128)S(1)}) fusion(bf16[3,3,1,128,128]{4,3,2,1,0:T(8,128)(2,1)S(1)} %get-tuple-element.21, bf16[3,3,1,128,128]{4,3,2,1,0:T(8,128)(2,1)S(1)} %get-tuple-element.20, bf16[3,3,1,128,128]{4,3,2,1,0:T(8,128)(2,1)S(1)} %get-tuple-element.19, ...), kind=kOutput, calls=%fused_computation.18 | convolution fusion | flops 6900842496 | bytes 12738584 | tf_op jit(solution)/shard_map/conv_general_dilated | solution.py:124
  100.0 3.9 %copy.41 = f32[18,18,8,3,128]{4,3,2,1,0:T(4,128)} copy(f32[18,18,8,3,128]{4,2,3,1,0:T(8,128)S(1)} %get-tuple-element.27) | data formatting | bytes 7962624 | tf_op jit(solution)/shard_map/conv_general_dilated | solution.py:124
  103.9 7.3 %reshape.117 = f32[18,18,1,24,128]{4,3,1,0,2:T(8,128)} reshape(f32[18,18,8,3,128]{4,3,2,1,0:T(4,128)} %copy.41) | data formatting | bytes 7962624 | tf_op jit(solution)/shard_map/conv_general_dilated | solution.py:124
  111.3 4.5 %slice_bitcast_fusion.1 = f32[18,18,18,128]{3,2,1,0:T(8,128)} fusion(f32[18,18,1,24,128]{4,3,1,0,2:T(8,128)} %reshape.117), kind=kLoop, calls=%fused_computation.17 | loop fusion | bytes 5971968 | tf_op jit(solution)/shard_map/squeeze | solution.py:124
  115.8 3.0 %add_divide_fusion = f32[18,18,18,128]{3,2,1,0:T(8,128)} fusion(f32[18,18,1,24,128]{4,3,1,0,2:T(8,128)S(1)} %copy-done.1), kind=kLoop, calls=%fused_computation.19 | loop fusion | flops 2239488 | bytes 5971968 | tf_op jit(solution)/shard_map/div | solution.py:173
  118.8 3.9 %convert_bitcast_fusion = f32[18,18,18,128]{3,2,1,0:T(8,128)} fusion(bf16[2,20,20,18,128]{4,3,2,1,0:T(8,128)(2,1)} %copy-done), kind=kLoop, calls=%fused_computation.5 | loop fusion | flops 746496 | bytes 4478976 | tf_op jit(solution)/shard_map/convert_element_type | solution.py:175
  122.7 3.9 %copy.43 = f32[18,18,8,3,128]{4,3,2,1,0:T(4,128)} copy(f32[18,18,8,3,128]{4,2,3,1,0:T(8,128)S(1)} %copy-done.10) | data formatting | bytes 7962624 | tf_op jit(solution)/shard_map/mul | solution.py:174
  126.6 7.3 %reshape.126 = f32[18,18,1,24,128]{4,3,1,0,2:T(8,128)} reshape(f32[18,18,8,3,128]{4,3,2,1,0:T(4,128)} %copy.43) | data formatting | bytes 7962624 | tf_op jit(solution)/shard_map/mul | solution.py:174
  133.9 3.2 %fusion.22 = bf16[18,18,1,18,128]{4,3,1,0,2:T(8,128)(2,1)S(1)} fusion(f32[18,18,1,24,128]{4,3,1,0,2:T(8,128)} %reshape.126, bf16[2,20,20,18,128]{4,3,2,1,0:T(8,128)(2,1)} %copy-done), kind=kLoop, calls=%fused_computation.34 | loop fusion | flops 2239488 | bytes 5971968 | tf_op jit(solution)/shard_map/convert_element_type | solution.py:175
  137.4 3.0 %reshape.120 = bf16[18,18,1,8,3,128]{5,4,3,1,0,2:T(4,128)(2,1)} reshape(bf16[18,18,1,24,128]{4,3,1,0,2:T(8,128)(2,1)S(1)} %pad.11) | data formatting | bytes 3981312 | tf_op jit(solution)/shard_map/conv_general_dilated | solution.py:124
  140.4 2.2 copy.45
  146.5 4.3 %fusion.31 = (bf16[1,16,16,16,128]{4,3,2,1,0:T(8,128)(2,1)S(1)}, f32[16,16,16,128]{3,2,1,0:T(8,128)}) fusion(f32[18,18,18,128]{3,2,1,0:T(8,128)S(1)} %copy-done.2, f32[18,18,18,128]{3,2,1,0:T(8,128)S(1)} %copy-done.3, f32[18,18,18,128]{3,2,1,0:T(8,128)} %convert_bitcast_fusion), kind=kLoop, calls=%fused_computation.42 | loop fusion | flops 3670016 | bytes 9437184 | tf_op jit(solution)/shard_map/broadcast_in_dim | solution.py:137
  150.8 32.2 %fusion.17 = f32[3,3,3,128,128]{4,3,2,1,0:T(8,128)S(1)} fusion(bf16[1,18,18,18,128]{4,3,2,1,0:T(8,128)(2,1)S(1)} %slice_bitcast_fusion.2, bf16[1,16,16,16,128]{4,3,2,1,0:T(8,128)(2,1)S(1)} %get-tuple-element.3), kind=kOutput, calls=%fused_computation.26 | convolution fusion | flops 3623878656 | bytes 4311040 | tf_op jit(solution)/shard_map/transpose | solution.py:143
  185.3 13.3 %fusion.25 = f32[16,16,8,3,128]{4,2,3,1,0:T(8,128)S(1)} fusion(bf16[18,18,1,7,2,128]{5,3,4,1,0,2:T(8,128)(2,1)S(1)} %copy-done.11, bf16[18,18,1,8,3,128]{5,3,4,1,0,2:T(8,128)(2,1)S(1)} %copy-done.8, pred[8,3]{0,1:T(4,128)(4,1)S(1)} %copy-done.19, bf16[3,3,1,128,128]{4,3,2,1,0:T(8,128)(2,1)} %copy-done.14, bf16[3,3,1,128,128]{4,3,2,1,0:T(8,128)(2,1)} %copy-done.13, ...), kind=kOutput, calls=%fused_computation.38 | convolution fusion | flops 5447442432 | bytes 7182360 | tf_op jit(solution)/shard_map/conv_general_dilated | solution.py:124
  199.4 1.6 copy.47
  201.0 2.0 copy.42
  203.0 7.8 %reduce-scatter.2.cloned.1.call-done = f32[27,16,64]{2,1,0:T(8,128)} async-done(((f32[27,64,64]{2,1,0:T(8,128)}), f32[27,16,64]{2,1,0:T(8,128)}) %reduce-scatter.2.cloned.1.call-update) | async-done | bytes 110608 | tf_op jit(solution)/shard_map/reduce_scatter | solution.py:187
  210.9 4.2 %multiply_convert_fusion = (bf16[1,16,8,8,512]{4,3,2,1,0:T(8,128)(2,1)}, bf16[1,16,8,8,512]{4,3,2,1,0:T(8,128)(2,1)}) fusion(f32[1,16,8,8,512]{4,3,2,1,0:T(8,128)S(1)} %bitcast.101, bf16[1,16,8,8,512]{4,3,2,1,0:T(8,128)(2,1)} %param.5, f32[16]{0:T(128)S(1)} %copy-done.17, f32[1,16,8,8,512]{4,3,2,1,0:T(8,128)} %bitcast.102, ...), kind=kLoop, calls=%fused_computation.30 | loop fusion | flops 4194304 | bytes 8388672 | tf_op jit(solution)/shard_map/convert_element_type | solution.py:181
  215.2 70.0 %all-reduce.7.cloned.1.call-done = f32[27,16,64]{2,1,0:T(8,128)} async-done(((f32[27,16,64]{2,1,0:T(8,128)}), f32[27,16,64]{2,1,0:T(8,128)}) %all-reduce.7.cloned.1.call-update) | async-done | bytes 110608 | tf_op jit(solution)/shard_map/psum | solution.py:188
  285.1 1.6 copy.61
  (85 shorter events, 21.0 us)
Async XLA Ops:
  7.2 12.6 %copy-start.18 = (s32[1,16]{1,0:T(1,128)S(1)}, s32[1,16]{1,0:T(1,128)}, u32[]{:S(2)}) copy-start(s32[1,16]{1,0:T(1,128)} %param.6) | copy-start | bytes 196
  7.2 4.9 %copy-start.15 = (bf16[27,16,64]{2,1,0:T(8,128)(2,1)S(1)}, bf16[27,16,64]{2,1,0:T(8,128)(2,1)}, u32[]{:S(2)}) copy-start(bf16[27,16,64]{2,1,0:T(8,128)(2,1)} %param.7) | copy-start | bytes 165892
  7.2 203.7 %reduce-scatter.2.cloned.1.call-start = ((), (), s32[]{:S(2)}) async-start(), calls=%async_computation.1 | async-start | bytes 1105920 | tf_op jit(solution)/shard_map/reduce_scatter | solution.py:187
  10.7 17.3 %collective-permute-start.1 = (bf16[2,2,16,16,128]{4,3,2,1,0:T(8,128)(2,1)S(1)}, bf16[2,2,16,16,128]{4,3,2,1,0:T(8,128)(2,1)S(1)}, u32[]{:S(2)}, u32[]{:S(2)}) collective-permute-start(bf16[2,2,16,16,128]{4,3,2,1,0:T(8,128)(2,1)S(1)} %get-tuple-element.12), channel_id=1, source_target_pairs={{16,0},{20,4},{24,8},{28,12},{17,1},{21,5},{25,9},{29,13},{18,2},{... | collective-permute-start | bytes 786440 | tf_op jit(solution)/shard_map/ppermute | solution.py:40
  12.1 27.2 %collective-permute-start.8 = (bf16[27,16,64]{2,1,0:T(8,128)(2,1)S(1)}, bf16[27,16,64]{2,1,0:T(8,128)(2,1)S(1)}, u32[]{:S(2)}, u32[]{:S(2)}) collective-permute-start(bf16[27,16,64]{2,1,0:T(8,128)(2,1)S(1)} %copy-done.15), channel_id=1, source_target_pairs={{1,0},{2,1},{3,2},{0,3},{5,4},{6,5},{7,6},{4,7},{9,8},{10,9},{11,1... | collective-permute-start | bytes 165896 | tf_op jit(solution)/shard_map/ppermute | solution.py:30
  14.5 15.8 %collective-permute-start.6 = (bf16[27,16,64]{2,1,0:T(8,128)(2,1)S(1)}, bf16[27,16,64]{2,1,0:T(8,128)(2,1)S(1)}, u32[]{:S(2)}, u32[]{:S(2)}) collective-permute-start(bf16[27,16,64]{2,1,0:T(8,128)(2,1)S(1)} %copy-done.15), channel_id=1, source_target_pairs={{0,1},{1,2},{2,3},{3,0},{4,5},{5,6},{6,7},{7,4},{8,9},{9,10},{10,1... | collective-permute-start | bytes 165896 | tf_op jit(solution)/shard_map/ppermute | solution.py:28
  14.5 13.5 %collective-permute-start = (bf16[2,2,16,16,128]{4,3,2,1,0:T(8,128)(2,1)S(1)}, bf16[2,2,16,16,128]{4,3,2,1,0:T(8,128)(2,1)S(1)}, u32[]{:S(2)}, u32[]{:S(2)}) collective-permute-start(bf16[2,2,16,16,128]{4,3,2,1,0:T(8,128)(2,1)S(1)} %get-tuple-element.11), channel_id=1, source_target_pairs={{0,16},{4,20},{8,24},{12,28},{1,17},{5,21},{9,25},{13,29},{2,18},{... | collective-permute-start | bytes 786440 | tf_op jit(solution)/shard_map/ppermute | solution.py:40
  29.0 15.6 %collective-permute-start.3 = (bf16[2,20,2,16,128]{4,3,2,1,0:T(8,128)(2,1)}, bf16[2,20,2,16,128]{4,3,2,1,0:T(8,128)(2,1)}, u32[]{:S(2)}, u32[]{:S(2)}) collective-permute-start(bf16[2,20,2,16,128]{4,3,2,1,0:T(8,128)(2,1)} %get-tuple-element.10), channel_id=1, source_target_pairs={{8,0},{12,4},{16,8},{20,12},{24,16},{28,20},{9,1},{13,5},{17,9},{2... | collective-permute-start | bytes 983048 | tf_op jit(solution)/shard_map/ppermute | solution.py:40
  30.3 8.9 %collective-permute-start.7 = (bf16[27,16,64]{2,1,0:T(8,128)(2,1)S(1)}, bf16[27,16,64]{2,1,0:T(8,128)(2,1)S(1)}, u32[]{:S(2)}, u32[]{:S(2)}) collective-permute-start(bf16[27,16,64]{2,1,0:T(8,128)(2,1)S(1)} %collective-permute-done.6), channel_id=1, source_target_pairs={{0,1},{1,2},{2,3},{3,0},{4,5},{5,6},{6,7},{7,4},{8,9},{9,10},{10,1... | collective-permute-start | bytes 165896 | tf_op jit(solution)/shard_map/ppermute | solution.py:28
  30.4 16.2 %collective-permute-start.2 = (bf16[2,20,2,16,128]{4,3,2,1,0:T(8,128)(2,1)}, bf16[2,20,2,16,128]{4,3,2,1,0:T(8,128)(2,1)}, u32[]{:S(2)}, u32[]{:S(2)}) collective-permute-start(bf16[2,20,2,16,128]{4,3,2,1,0:T(8,128)(2,1)} %get-tuple-element.9), channel_id=1, source_target_pairs={{0,8},{4,12},{8,16},{12,20},{16,24},{20,28},{1,9},{5,13},{9,17},{1... | collective-permute-start | bytes 983048 | tf_op jit(solution)/shard_map/ppermute | solution.py:40
  39.2 0.6 copy-start.16
  48.6 13.6 %collective-permute-start.5 = (bf16[2,20,20,1,128]{4,3,2,1,0:T(2,128)(2,1)S(1)}, bf16[2,20,20,1,128]{4,3,2,1,0:T(2,128)(2,1)S(1)}, u32[]{:S(2)}, u32[]{:S(2)}) collective-permute-start(bf16[2,20,20,1,128]{4,3,2,1,0:T(2,128)(2,1)S(1)} %get-tuple-element.8), channel_id=1, source_target_pairs={{4,0},{8,4},{12,8},{16,12},{20,16},{24,20},{28,24},{5,1},{9,5},{13... | collective-permute-start | bytes 614408 | tf_op jit(solution)/shard_map/ppermute | solution.py:40
  50.2 32.5 %copy-start.12 = (bf16[3,3,1,128,128]{4,3,2,1,0:T(8,128)(2,1)}, bf16[3,3,1,128,128]{4,3,2,1,0:T(8,128)(2,1)S(1)}, u32[]{:S(2)}) copy-start(bf16[3,3,1,128,128]{4,3,2,1,0:T(8,128)(2,1)S(1)} %get-tuple-element.19) | copy-start | bytes 884740
  50.2 32.5 %copy-start.13 = (bf16[3,3,1,128,128]{4,3,2,1,0:T(8,128)(2,1)}, bf16[3,3,1,128,128]{4,3,2,1,0:T(8,128)(2,1)S(1)}, u32[]{:S(2)}) copy-start(bf16[3,3,1,128,128]{4,3,2,1,0:T(8,128)(2,1)S(1)} %get-tuple-element.20) | copy-start | bytes 884740
  50.3 32.5 %copy-start.14 = (bf16[3,3,1,128,128]{4,3,2,1,0:T(8,128)(2,1)}, bf16[3,3,1,128,128]{4,3,2,1,0:T(8,128)(2,1)S(1)}, u32[]{:S(2)}) copy-start(bf16[3,3,1,128,128]{4,3,2,1,0:T(8,128)(2,1)S(1)} %get-tuple-element.21) | copy-start | bytes 884740
  50.3 21.2 %collective-permute-start.4 = (bf16[2,20,20,1,128]{4,3,2,1,0:T(2,128)(2,1)S(1)}, bf16[2,20,20,1,128]{4,3,2,1,0:T(2,128)(2,1)S(1)}, u32[]{:S(2)}, u32[]{:S(2)}) collective-permute-start(bf16[2,20,20,1,128]{4,3,2,1,0:T(2,128)(2,1)S(1)} %get-tuple-element.7), channel_id=1, source_target_pairs={{0,4},{4,8},{8,12},{12,16},{16,20},{20,24},{24,28},{1,5},{5,9},{9,... | collective-permute-start | bytes 614408 | tf_op jit(solution)/shard_map/ppermute | solution.py:40
  77.8 3.0 %copy-start = (bf16[2,20,20,18,128]{4,3,2,1,0:T(8,128)(2,1)}, bf16[2,20,20,18,128]{4,3,2,1,0:T(8,128)(2,1)S(1)}, u32[]{:S(2)}) copy-start(bf16[2,20,20,18,128]{4,3,2,1,0:T(8,128)(2,1)S(1)} %pad_maximum_fusion) | copy-start | bytes 11059204
  81.9 0.8 copy-start.20
  111.3 4.5 %copy-start.1 = (f32[18,18,1,24,128]{4,3,1,0,2:T(8,128)S(1)}, f32[18,18,1,24,128]{4,3,1,0,2:T(8,128)}, u32[]{:S(2)}) copy-start(f32[18,18,1,24,128]{4,3,1,0,2:T(8,128)} %reshape.117) | copy-start | bytes 11943940
  118.8 3.9 %copy-start.10 = (f32[18,18,8,3,128]{4,2,3,1,0:T(8,128)S(1)}, f32[18,18,8,3,128]{4,2,3,1,0:T(8,128)}, u32[]{:S(2)}) copy-start(f32[18,18,8,3,128]{4,2,3,1,0:T(8,128)} %get-tuple-element.26) | copy-start | bytes 11943940
  140.4 3.7 %copy-start.6 = (bf16[20,20,20,128]{3,2,1,0:T(8,128)(2,1)S(1)}, bf16[20,20,20,128]{3,2,1,0:T(8,128)(2,1)}, u32[]{:S(2)}) copy-start(bf16[20,20,20,128]{3,2,1,0:T(8,128)(2,1)} %get-tuple-element.5) | copy-start | bytes 6144004
  140.4 4.9 %copy-start.3 = (f32[18,18,18,128]{3,2,1,0:T(8,128)S(1)}, f32[18,18,18,128]{3,2,1,0:T(8,128)}, u32[]{:S(2)}) copy-start(f32[18,18,18,128]{3,2,1,0:T(8,128)} %add_divide_fusion) | copy-start | bytes 8957956
  142.7 8.1 %copy-start.7 = (bf16[18,18,1,8,3,128]{5,3,4,1,0,2:T(8,128)(2,1)}, bf16[18,18,1,8,3,128]{5,3,4,1,0,2:T(8,128)(2,1)S(1)}, u32[]{:S(2)}) copy-start(bf16[18,18,1,8,3,128]{5,3,4,1,0,2:T(8,128)(2,1)S(1)} %copy.45) | copy-start | bytes 5971972
  142.7 3.8 %copy-start.2 = (f32[18,18,18,128]{3,2,1,0:T(8,128)S(1)}, f32[18,18,18,128]{3,2,1,0:T(8,128)}, u32[]{:S(2)}) copy-start(f32[18,18,18,128]{3,2,1,0:T(8,128)} %slice_bitcast_fusion.1) | copy-start | bytes 8957956
  183.0 1.9 copy-start.8
  183.1 2.2 copy-start.11
  183.1 2.2 copy-start.19
  184.4 100.7 %all-reduce.7.cloned.1.call-start = ((), (), s32[]{:S(2)}) async-start(), calls=%async_computation.2 | async-start | bytes 442368 | tf_op jit(solution)/shard_map/psum | solution.py:188
  199.2 1.9 copy-start.4
  199.4 11.5 %copy-start.9 = (bf16[1,16,8,8,512]{4,3,2,1,0:T(8,128)(2,1)S(1)}, bf16[1,16,8,8,512]{4,3,2,1,0:T(8,128)(2,1)}, u32[]{:S(2)}) copy-start(bf16[1,16,8,8,512]{4,3,2,1,0:T(8,128)(2,1)} %param.4) | copy-start | bytes 3145732
  199.4 11.5 %copy-start.17 = (f32[16]{0:T(128)S(1)}, f32[16]{0:T(128)}, u32[]{:S(2)}) copy-start(f32[16]{0:T(128)} %convert_bitcast_fusion.1) | copy-start | bytes 196
  201.0 9.9 %copy-start.5 = (f32[2,2,4,8,8,4,128]{6,4,5,3,2,1,0:T(8,128)S(1)}, f32[2,2,4,8,8,4,128]{6,4,5,3,2,1,0:T(8,128)}, u32[]{:S(2)}) copy-start(f32[2,2,4,8,8,4,128]{6,4,5,3,2,1,0:T(8,128)} %copy.47) | copy-start | bytes 6291460
Sparse Core Ops, SparseCore 0:
  184.5 26.2 reduce-scatter.1
  214.2 70.8 all-reduce.6
